TPU v7x, 512 devices: a whole 4x8x8 slice. The times are simulated.
512 devices in a mesh: ctx: 32 (over z, x), exp: 16 (over y, core).
Axes of the slice: x: 4, y: 8, z: 8, core: 2. Of those that a mesh axis runs over, the one named last changes fastest.
Arguments:
- stream: bfloat16 [16, 4096, 1024], P('exp', 'ctx'), may hold values from -400 to 400
- queries: bfloat16 [16, 4096, 16, 128], P('exp', 'ctx'), may hold values from -6 to 6
- key_rows: bfloat16 [16, 4096, 2, 128], P('exp', 'ctx'), may hold values from -4 to 4
- value_rows: bfloat16 [16, 4096, 2, 128], P('exp', 'ctx'), may hold values from -6 to 6
- expert_ids: int32 [16, 4096, 2], P('exp', 'ctx'), may hold values from 0 to 127, as said below
- norm_gain: bfloat16 [1024], replicated, may hold values from 0.099609375 to 1.8984375
- router_weight: bfloat16 [1024, 128], replicated, may hold values from -0.1875 to 0.1875
- gate_weight: bfloat16 [98304, 1024], P(('ctx', 'exp')), may hold values from -0.1875 to 0.1875
- up_weight: bfloat16 [98304, 1024], P(('ctx', 'exp')), may hold values from -0.1875 to 0.1875
- down_weight: bfloat16 [98304, 1024], P(('ctx', 'exp')), may hold values from -0.21875 to 0.21875
Outputs:
- attended: bfloat16 [16, 4096, 16, 128], P('exp', 'ctx')
- expert_mix: bfloat16 [16, 4096, 1024], P('exp', 'ctx')
Inputs may be any that keep to these rules, and one draw needn't show every extreme that they name: `expert_ids`: within the rows of one device (aligned blocks of 128 positions of one sequence), a token's 2 experts differ and no expert is named more than 4 times; one expert is named exactly 4 times in every such block.
All inputs are finite; a program needn't handle non-finite values.
Results may differ from a plain program's by a relative error of at most 0.01.
Values may be sent and summed in bfloat16 or wider, within the bound.
No kernel may reach another device: no remote copies, remote signals or barrier semaphores. Data moves between devices by JAX's collectives and lax.ppermute only.
A program may use at most 64 MiB of HBM per device.

v0:
```python
import math
import jax
import jax.numpy as jnp
from jax import lax
from jax.sharding import PartitionSpec as P


def from_partner(value, axis, bit):
    return lax.ppermute(value, axis, [(i, i ^ 1 << bit) for i in range(lax.axis_size(axis))])


def expert_rows(inputs, gate_rows, up_rows, down_rows):
    features = inputs.shape[-1]
    flat_rows = inputs.reshape(-1, features)
    contract = (((1,), (1,)), ((), ()))
    gate_part = lax.dot_general(flat_rows, gate_rows, contract, preferred_element_type=jnp.float32)
    up_part = lax.dot_general(flat_rows, up_rows, contract, preferred_element_type=jnp.float32)
    hidden = (jax.nn.silu(gate_part) * up_part).astype(jnp.bfloat16)
    projected = jnp.dot(hidden, down_rows, preferred_element_type=jnp.float32)
    return projected.reshape(inputs.shape)


def attention(queries, key_rows, value_rows):
    seq_rows = queries.shape[1]
    head_count = queries.shape[2]
    head_size = queries.shape[3]
    kv_count = key_rows.shape[2]
    group_size = head_count // kv_count
    grouped = queries[0].reshape(seq_rows, kv_count, group_size, head_size)
    scaling = 1.0 / math.sqrt(head_size)
    query_pos = lax.axis_index("ctx") * seq_rows + jnp.arange(seq_rows, dtype=jnp.int32)
    initial = (
        jnp.full((kv_count, group_size, seq_rows), -1e30, jnp.float32),
        jnp.zeros((kv_count, group_size, seq_rows), jnp.float32),
        jnp.zeros((kv_count, group_size, seq_rows, head_size), jnp.float32),
    )
    key_piece = lax.all_gather(key_rows, "ctx", axis=1, tiled=True)
    value_piece = lax.all_gather(value_rows, "ctx", axis=1, tiled=True)
    piece_rows = key_piece.shape[1]
    block_rows = math.gcd(piece_rows, 512)
    block_count = piece_rows // block_rows
    key_blocks = key_piece[0].reshape(block_count, block_rows, kv_count, head_size)
    value_blocks = value_piece[0].reshape(block_count, block_rows, kv_count, head_size)

    def advance(status, members):
        running, totals, accumulated = status
        key_block, value_block, offset = members
        scores = (
            jnp.einsum("qhgd,khd->hgqk", grouped, key_block, preferred_element_type=jnp.float32)
            * scaling
        )
        key_pos = offset * block_rows + jnp.arange(block_rows, dtype=jnp.int32)
        visible = key_pos[None, :] <= query_pos[:, None]
        scores = jnp.where(visible, scores, -1e30)
        highest = jnp.maximum(running, jnp.max(scores, axis=-1))
        factor = jnp.exp(running - highest)
        weights = jnp.where(visible, jnp.exp(scores - highest[..., None]), 0.0)
        totals = totals * factor + jnp.sum(weights, axis=-1)
        accumulated = accumulated * factor[..., None] + jnp.einsum(
            "hgqk,khd->hgqd",
            weights.astype(jnp.bfloat16),
            value_block,
            preferred_element_type=jnp.float32,
        )
        return ((highest, totals, accumulated), None)

    status, unused = lax.scan(
        advance, initial, (key_blocks, value_blocks, jnp.arange(block_count, dtype=jnp.int32))
    )
    running, totals, accumulated = status
    result = accumulated / totals[..., None]
    return (
        jnp.transpose(result, (2, 0, 1, 3))
        .reshape(1, seq_rows, head_count, head_size)
        .astype(jnp.bfloat16)
    )


def local(
    stream,
    queries,
    key_rows,
    value_rows,
    expert_ids,
    norm_gain,
    router_weight,
    gate_weight,
    up_weight,
    down_weight,
):
    attended = attention(queries, key_rows, value_rows)
    ctx_count = lax.axis_size("ctx")
    exp_count = lax.axis_size("exp")
    tokens = stream.shape[1]
    features = stream.shape[2]
    top_count = expert_ids.shape[2]
    expert_total = router_weight.shape[1]
    per_ctx = expert_total // ctx_count
    quarters = exp_count // per_ctx
    capacity = 2 * tokens * top_count // expert_total
    widened = stream[0].astype(jnp.float32)
    mean_square = jnp.mean(widened * widened, axis=-1, keepdims=True)
    normed = (widened * lax.rsqrt(mean_square + 1e-06) * norm_gain.astype(jnp.float32)).astype(
        jnp.bfloat16
    )
    logits = jnp.dot(normed, router_weight, preferred_element_type=jnp.float32)
    chosen = expert_ids[0]
    gate_values = jax.nn.sigmoid(jnp.take_along_axis(logits, chosen, axis=1))
    flat_ids = chosen.reshape(-1)
    onehot = (flat_ids[:, None] == jnp.arange(expert_total, dtype=jnp.int32)[None, :]).astype(
        jnp.int32
    )
    earlier = jnp.cumsum(onehot, axis=0) - onehot
    slot_index = jnp.sum(earlier * onehot, axis=1)
    target = (flat_ids % per_ctx * ctx_count + flat_ids // per_ctx) * capacity + slot_index
    source_rows = jnp.repeat(normed, top_count, axis=0)
    outgoing = (
        jnp.zeros((expert_total * capacity, features), jnp.bfloat16).at[target].set(source_rows)
    )
    outgoing = outgoing.reshape(per_ctx, ctx_count, capacity, features)
    arrived = lax.all_to_all(outgoing, "ctx", split_axis=1, concat_axis=1, tiled=True)
    stacked = jnp.stack([gate_weight, up_weight, down_weight], axis=0)
    my_exp = lax.axis_index("exp")
    partner = from_partner(stacked, "exp", 0)
    upper_side = my_exp & 1 == 1
    held = jnp.where(
        upper_side,
        jnp.concatenate([partner, stacked], axis=1),
        jnp.concatenate([stacked, partner], axis=1),
    )
    half_ctx = ctx_count // 2
    halves_rows = arrived.reshape(per_ctx, 1, 2, half_ctx, capacity, features)
    spread_rows = jnp.broadcast_to(
        halves_rows, (per_ctx, quarters // 2, 2, half_ctx, capacity, features)
    )
    spread_rows = spread_rows.reshape(exp_count, half_ctx, capacity, features)
    received = lax.all_to_all(spread_rows, "exp", split_axis=0, concat_axis=0, tiled=True)
    partials = expert_rows(received, held[0], held[1], held[2])
    returned = lax.all_to_all(
        partials.astype(jnp.bfloat16), "exp", split_axis=0, concat_axis=0, tiled=True
    ).astype(partials.dtype)
    summed = jnp.sum(
        returned.reshape(per_ctx, quarters // 2, 2, half_ctx, capacity, features), axis=1
    )
    finished = summed.astype(jnp.bfloat16).reshape(per_ctx, ctx_count, capacity, features)
    came_back = lax.all_to_all(finished, "ctx", split_axis=1, concat_axis=1, tiled=True)
    flat_back = came_back.reshape(expert_total * capacity, features)
    picked = (
        jnp.take(flat_back, target, axis=0).astype(jnp.float32).reshape(tokens, top_count, features)
    )
    mixture = jnp.sum(picked * gate_values[:, :, None], axis=1).astype(jnp.bfloat16)
    return (attended, mixture[None])


def solution(mesh):
    placed = (
        P("exp", "ctx", None),
        P("exp", "ctx", None, None),
        P("exp", "ctx", None, None),
        P("exp", "ctx", None, None),
        P("exp", "ctx", None),
        P(),
        P(),
        P(("ctx", "exp"), None),
        P(("ctx", "exp"), None),
        P(("ctx", "exp"), None),
    )
    return jax.shard_map(
        local,
        mesh=mesh,
        in_specs=placed,
        out_specs=(P("exp", "ctx", None, None), P("exp", "ctx", None)),
        check_vma=False,
    )
```

profile of v0, /device:TPU:16, one launch (start us, length us, event | category | flops | bytes accessed | tf_op | source)
XLA Modules:
  0.0 309.8 jit_solution(2212090198150793443)
XLA Ops:
  16.4 13.2 %all-to-all-start = ((bf16[4,32,4,1024]{3,2,0,1:T(4,128)(2,1)}), bf16[4,32,4,1024]{3,2,0,1:T(4,128)(2,1)S(1)}, u32[]{:S(2)}, u32[]{:S(2)}) async-start(bf16[4,32,4,1024]{3,2,0,1:T(4,128)(2,1)} %copy.84), calls=%async_computation | async-start | bytes 2097152 | tf_op jit(solution)/shard_map/all_to_all | solution.py:121
  30.3 27.4 %all-to-all-done = bf16[4,32,4,1024]{3,2,0,1:T(4,128)(2,1)S(1)} async-done(((bf16[4,32,4,1024]{3,2,0,1:T(4,128)(2,1)}), bf16[4,32,4,1024]{3,2,0,1:T(4,128)(2,1)S(1)}, u32[]{:S(2)}, u32[]{:S(2)}) %all-to-all-start) | async-done | bytes 1048608 | tf_op jit(solution)/shard_map/all_to_all | solution.py:121
  60.2 7.6 %all-to-all-start.1 = ((bf16[16,16,4,1024]{3,2,1,0:T(4,128)(2,1)}), bf16[16,16,4,1024]{3,2,1,0:T(4,128)(2,1)S(1)}, u32[]{:S(2)}, u32[]{:S(2)}) async-start(bf16[16,16,4,1024]{3,2,1,0:T(4,128)(2,1)} %bitcast.120), calls=%async_computation.1 | async-start | bytes 4194304 | tf_op jit(solution)/shard_map/all_to_all | solution.py:137
  75.1 3.5 %maximum_select_fusion = bf16[3,384,1024]{2,1,0:T(8,128)(2,1)} fusion(bf16[1,192,1024]{2,1,0:T(8,128)(2,1)S(1)} %bitcast.124, bf16[1,192,1024]{2,1,0:T(8,128)(2,1)S(1)} %bitcast.126, bf16[1,192,1024]{2,1,0:T(8,128)(2,1)} %bitcast.128, bf16[3,192,1024]{2,1,0:T(8,128)(2,1)} %collective-permute-done, pred[]{:T(512)S(6)} %eq.35), kind=kLoop, calls=%fused_computation.30 | loop fusion | flops 20054016 | bytes 4718593 | tf_op jit(solution)/shard_map/jit(_where)/select_n | solution.py:126
  78.6 36.6 %all-to-all-done.1 = bf16[16,16,4,1024]{3,2,1,0:T(4,128)(2,1)S(1)} async-done(((bf16[16,16,4,1024]{3,2,1,0:T(4,128)(2,1)}), bf16[16,16,4,1024]{3,2,1,0:T(4,128)(2,1)S(1)}, u32[]{:S(2)}, u32[]{:S(2)}) %all-to-all-start.1) | async-done | bytes 2097184 | tf_op jit(solution)/shard_map/all_to_all | solution.py:137
  125.1 3.7 %convolution_convert_fusion = bf16[16,16,4,1024]{3,1,2,0:T(8,128)(2,1)} fusion(bf16[3,384,1024]{2,1,0:T(8,128)(2,1)S(1)} %copy-done.2, bf16[16,16,4,384]{3,2,1,0:T(4,128)(2,1)} %dot_general.22), kind=kOutput, calls=%fused_computation.31 | convolution fusion | flops 806354944 | bytes 3670016 | tf_op jit(solution)/shard_map/dot_general | solution.py:19
  128.8 6.7 %all-to-all-start.2 = ((bf16[16,16,4,1024]{3,1,2,0:T(8,128)(2,1)}), bf16[16,16,4,1024]{3,1,2,0:T(8,128)(2,1)S(1)}, u32[]{:S(2)}, u32[]{:S(2)}) async-start(bf16[16,16,4,1024]{3,1,2,0:T(8,128)(2,1)} %convolution_convert_fusion), calls=%async_computation.2 | async-start | bytes 4194304 | tf_op jit(solution)/shard_map/all_to_all | solution.py:139
  139.9 43.0 %all-to-all-done.2 = bf16[16,16,4,1024]{3,1,2,0:T(8,128)(2,1)S(1)} async-done(((bf16[16,16,4,1024]{3,1,2,0:T(8,128)(2,1)}), bf16[16,16,4,1024]{3,1,2,0:T(8,128)(2,1)S(1)}, u32[]{:S(2)}, u32[]{:S(2)}) %all-to-all-start.2) | async-done | bytes 2097184 | tf_op jit(solution)/shard_map/all_to_all | solution.py:139
  187.7 5.3 %all-to-all-start.3 = ((bf16[4,32,4,1024]{3,2,0,1:T(4,128)(2,1)}), bf16[4,32,4,1024]{3,2,0,1:T(4,128)(2,1)S(1)}, u32[]{:S(2)}, u32[]{:S(2)}) async-start(bf16[4,32,4,1024]{3,2,0,1:T(4,128)(2,1)} %copy.88), calls=%async_computation.3 | async-start | bytes 2097152 | tf_op jit(solution)/shard_map/all_to_all | solution.py:146
  193.1 14.3 %all-gather.5.cloned.1.call-done = bf16[1,4096,2,128]{3,1,2,0:T(8,128)(2,1)} async-done(((bf16[1,128,2,128]{3,1,2,0:T(8,128)(2,1)}), bf16[1,4096,2,128]{3,1,2,0:T(8,128)(2,1)}) %all-gather.5.cloned.1.call-update) | async-done | bytes 2097168 | tf_op jit(solution)/shard_map/all_gather | solution.py:38
  207.4 89.6 %while.15 = (s32[]{:T(128)}, f32[2,8,128]{2,1,0:T(8,128)S(1)}, f32[2,8,128]{2,1,0:T(8,128)S(1)}, f32[2,8,128,128]{3,2,1,0:T(8,128)S(1)}, s32[8]{0:T(128)S(1)}, /...) while((s32[]{:T(128)}, f32[2,8,128]{2,1,0:T(8,128)S(1)}, ...), condition=%wide.region_3.4_spmd.clone, body=%wide.region_0.3_spmd.clone.sunk | while | flops 551365248 | bytes 32904396 | solution.py:67
  208.8 3.7 %fusion.58 = (f32[2,8,128]{2,1,0:T(8,128)S(1)}, f32[2,512,128,8]{2,1,3,0:T(8,128)}) fusion(pred[128,512]{0,1:T(8,128)(4,1)S(1)} %broadcast_compare_fusion.2, bf16[128,2,8,128]{3,0,2,1:T(8,128)(2,1)S(1)} %get-tuple-element.236, bf16[8,512,2,128]{3,1,0,2:T(8,128)(2,1)} %get-tuple-element.235, s32[]{:T(128)S(6)} %copy.107), kind=kOutput, calls=%fused_computation.6.clone.1 | convolution fusion | flops 271579136 | bytes 5054468 | tf_op jit(solution)/shard_map/while/body/eval_jaxpr/qhgd,khd->hgqk/dot_general | solution.py:49
  212.5 3.3 %fusion.59 = f32[2,8,128]{2,1,0:T(8,128)S(1)} fusion(f32[2,512,128,8]{2,1,3,0:T(8,128)} %get-tuple-element.203, f32[2,8,128]{2,1,0:T(8,128)S(1)} %select_maximum_fusion.2, pred[128,512]{0,1:T(8,128)(4,1)S(1)} %broadcast_compare_fusion.2), kind=kLoop, calls=%fused_computation.8.clone.1 | loop fusion | flops 5240832 | bytes 4276224 | tf_op jit(solution)/shard_map/while/body/eval_jaxpr/reduce_sum | solution.py:58
  220.0 3.7 %fusion.58 = (f32[2,8,128]{2,1,0:T(8,128)S(1)}, f32[2,512,128,8]{2,1,3,0:T(8,128)}) fusion(pred[128,512]{0,1:T(8,128)(4,1)S(1)} %broadcast_compare_fusion.2, bf16[128,2,8,128]{3,0,2,1:T(8,128)(2,1)S(1)} %get-tuple-element.236, bf16[8,512,2,128]{3,1,0,2:T(8,128)(2,1)} %get-tuple-element.235, s32[]{:T(128)S(6)} %copy.107), kind=kOutput, calls=%fused_computation.6.clone.1 | convolution fusion | flops 271579136 | bytes 5054468 | tf_op jit(solution)/shard_map/while/body/eval_jaxpr/qhgd,khd->hgqk/dot_general | solution.py:49
  223.7 3.3 %fusion.59 = f32[2,8,128]{2,1,0:T(8,128)S(1)} fusion(f32[2,512,128,8]{2,1,3,0:T(8,128)} %get-tuple-element.203, f32[2,8,128]{2,1,0:T(8,128)S(1)} %select_maximum_fusion.2, pred[128,512]{0,1:T(8,128)(4,1)S(1)} %broadcast_compare_fusion.2), kind=kLoop, calls=%fused_computation.8.clone.1 | loop fusion | flops 5240832 | bytes 4276224 | tf_op jit(solution)/shard_map/while/body/eval_jaxpr/reduce_sum | solution.py:58
  231.2 3.7 %fusion.58 = (f32[2,8,128]{2,1,0:T(8,128)S(1)}, f32[2,512,128,8]{2,1,3,0:T(8,128)}) fusion(pred[128,512]{0,1:T(8,128)(4,1)S(1)} %broadcast_compare_fusion.2, bf16[128,2,8,128]{3,0,2,1:T(8,128)(2,1)S(1)} %get-tuple-element.236, bf16[8,512,2,128]{3,1,0,2:T(8,128)(2,1)} %get-tuple-element.235, s32[]{:T(128)S(6)} %copy.107), kind=kOutput, calls=%fused_computation.6.clone.1 | convolution fusion | flops 271579136 | bytes 5054468 | tf_op jit(solution)/shard_map/while/body/eval_jaxpr/qhgd,khd->hgqk/dot_general | solution.py:49
  234.9 3.3 %fusion.59 = f32[2,8,128]{2,1,0:T(8,128)S(1)} fusion(f32[2,512,128,8]{2,1,3,0:T(8,128)} %get-tuple-element.203, f32[2,8,128]{2,1,0:T(8,128)S(1)} %select_maximum_fusion.2, pred[128,512]{0,1:T(8,128)(4,1)S(1)} %broadcast_compare_fusion.2), kind=kLoop, calls=%fused_computation.8.clone.1 | loop fusion | flops 5240832 | bytes 4276224 | tf_op jit(solution)/shard_map/while/body/eval_jaxpr/reduce_sum | solution.py:58
  242.5 3.7 %fusion.58 = (f32[2,8,128]{2,1,0:T(8,128)S(1)}, f32[2,512,128,8]{2,1,3,0:T(8,128)}) fusion(pred[128,512]{0,1:T(8,128)(4,1)S(1)} %broadcast_compare_fusion.2, bf16[128,2,8,128]{3,0,2,1:T(8,128)(2,1)S(1)} %get-tuple-element.236, bf16[8,512,2,128]{3,1,0,2:T(8,128)(2,1)} %get-tuple-element.235, s32[]{:T(128)S(6)} %copy.107), kind=kOutput, calls=%fused_computation.6.clone.1 | convolution fusion | flops 271579136 | bytes 5054468 | tf_op jit(solution)/shard_map/while/body/eval_jaxpr/qhgd,khd->hgqk/dot_general | solution.py:49
  246.1 3.3 %fusion.59 = f32[2,8,128]{2,1,0:T(8,128)S(1)} fusion(f32[2,512,128,8]{2,1,3,0:T(8,128)} %get-tuple-element.203, f32[2,8,128]{2,1,0:T(8,128)S(1)} %select_maximum_fusion.2, pred[128,512]{0,1:T(8,128)(4,1)S(1)} %broadcast_compare_fusion.2), kind=kLoop, calls=%fused_computation.8.clone.1 | loop fusion | flops 5240832 | bytes 4276224 | tf_op jit(solution)/shard_map/while/body/eval_jaxpr/reduce_sum | solution.py:58
  253.7 3.7 %fusion.58 = (f32[2,8,128]{2,1,0:T(8,128)S(1)}, f32[2,512,128,8]{2,1,3,0:T(8,128)}) fusion(pred[128,512]{0,1:T(8,128)(4,1)S(1)} %broadcast_compare_fusion.2, bf16[128,2,8,128]{3,0,2,1:T(8,128)(2,1)S(1)} %get-tuple-element.236, bf16[8,512,2,128]{3,1,0,2:T(8,128)(2,1)} %get-tuple-element.235, s32[]{:T(128)S(6)} %copy.107), kind=kOutput, calls=%fused_computation.6.clone.1 | convolution fusion | flops 271579136 | bytes 5054468 | tf_op jit(solution)/shard_map/while/body/eval_jaxpr/qhgd,khd->hgqk/dot_general | solution.py:49
  264.9 3.7 %fusion.58 = (f32[2,8,128]{2,1,0:T(8,128)S(1)}, f32[2,512,128,8]{2,1,3,0:T(8,128)}) fusion(pred[128,512]{0,1:T(8,128)(4,1)S(1)} %broadcast_compare_fusion.2, bf16[128,2,8,128]{3,0,2,1:T(8,128)(2,1)S(1)} %get-tuple-element.236, bf16[8,512,2,128]{3,1,0,2:T(8,128)(2,1)} %get-tuple-element.235, s32[]{:T(128)S(6)} %copy.107), kind=kOutput, calls=%fused_computation.6.clone.1 | convolution fusion | flops 271579136 | bytes 5054468 | tf_op jit(solution)/shard_map/while/body/eval_jaxpr/qhgd,khd->hgqk/dot_general | solution.py:49
  276.1 3.7 %fusion.58 = (f32[2,8,128]{2,1,0:T(8,128)S(1)}, f32[2,512,128,8]{2,1,3,0:T(8,128)}) fusion(pred[128,512]{0,1:T(8,128)(4,1)S(1)} %broadcast_compare_fusion.2, bf16[128,2,8,128]{3,0,2,1:T(8,128)(2,1)S(1)} %get-tuple-element.236, bf16[8,512,2,128]{3,1,0,2:T(8,128)(2,1)} %get-tuple-element.235, s32[]{:T(128)S(6)} %copy.107), kind=kOutput, calls=%fused_computation.6.clone.1 | convolution fusion | flops 271579136 | bytes 5054468 | tf_op jit(solution)/shard_map/while/body/eval_jaxpr/qhgd,khd->hgqk/dot_general | solution.py:49
  287.3 3.7 %fusion.58 = (f32[2,8,128]{2,1,0:T(8,128)S(1)}, f32[2,512,128,8]{2,1,3,0:T(8,128)}) fusion(pred[128,512]{0,1:T(8,128)(4,1)S(1)} %broadcast_compare_fusion.2, bf16[128,2,8,128]{3,0,2,1:T(8,128)(2,1)S(1)} %get-tuple-element.236, bf16[8,512,2,128]{3,1,0,2:T(8,128)(2,1)} %get-tuple-element.235, s32[]{:T(128)S(6)} %copy.107), kind=kOutput, calls=%fused_computation.6.clone.1 | convolution fusion | flops 271579136 | bytes 5054468 | tf_op jit(solution)/shard_map/while/body/eval_jaxpr/qhgd,khd->hgqk/dot_general | solution.py:49
  291.0 3.3 %fusion.59 = f32[2,8,128]{2,1,0:T(8,128)S(1)} fusion(f32[2,512,128,8]{2,1,3,0:T(8,128)} %get-tuple-element.203, f32[2,8,128]{2,1,0:T(8,128)S(1)} %select_maximum_fusion.2, pred[128,512]{0,1:T(8,128)(4,1)S(1)} %broadcast_compare_fusion.2), kind=kLoop, calls=%fused_computation.8.clone.1 | loop fusion | flops 5240832 | bytes 4276224 | tf_op jit(solution)/shard_map/while/body/eval_jaxpr/reduce_sum | solution.py:58
  (170 shorter events, 82.4 us)
Async XLA Ops:
  7.2 130.2 %copy-start = (bf16[1024,128]{1,0:T(8,128)(2,1)S(1)}, bf16[1024,128]{1,0:T(8,128)(2,1)}, u32[]{:S(2)}) copy-start(bf16[1024,128]{1,0:T(8,128)(2,1)} %param.18) | copy-start | bytes 786436
  14.8 14.8 %copy-start.7 = (bf16[1,128,2,128]{3,2,1,0:T(2,128)(2,1)S(1)}, bf16[1,128,2,128]{3,2,1,0:T(2,128)(2,1)}, u32[]{:S(2)}) copy-start(bf16[1,128,2,128]{3,2,1,0:T(2,128)(2,1)} %param.14) | copy-start | bytes 196612
  16.4 41.3 %all-to-all-start = ((bf16[4,32,4,1024]{3,2,0,1:T(4,128)(2,1)}), bf16[4,32,4,1024]{3,2,0,1:T(4,128)(2,1)S(1)}, u32[]{:S(2)}, u32[]{:S(2)}) async-start(bf16[4,32,4,1024]{3,2,0,1:T(4,128)(2,1)} %copy.84), calls=%async_computation | async-start | bytes 2097152 | tf_op jit(solution)/shard_map/all_to_all | solution.py:121
  29.5 163.6 %all-gather.3.cloned.1.call-start = ((), (), s32[]{:S(2)}) async-start(), calls=%async_computation.4 | async-start | bytes 2162688 | tf_op jit(solution)/shard_map/all_gather | solution.py:37
  60.2 7.6 %copy-start.4 = (bf16[192,1024]{1,0:T(8,128)(2,1)S(1)}, bf16[192,1024]{1,0:T(8,128)(2,1)}, u32[]{:S(2)}) copy-start(bf16[192,1024]{1,0:T(8,128)(2,1)} %param.21) | copy-start | bytes 1179652
  60.2 7.6 %copy-start.5 = (bf16[192,1024]{1,0:T(8,128)(2,1)S(1)}, bf16[192,1024]{1,0:T(8,128)(2,1)}, u32[]{:S(2)}) copy-start(bf16[192,1024]{1,0:T(8,128)(2,1)} %param.20) | copy-start | bytes 1179652
  60.2 11.9 %copy-start.8 = (bf16[1,128,2,128]{3,2,1,0:T(2,128)(2,1)S(1)}, bf16[1,128,2,128]{3,2,1,0:T(2,128)(2,1)}, u32[]{:S(2)}) copy-start(bf16[1,128,2,128]{3,2,1,0:T(2,128)(2,1)} %param.15) | copy-start | bytes 196612
  60.2 55.0 %all-to-all-start.1 = ((bf16[16,16,4,1024]{3,2,1,0:T(4,128)(2,1)}), bf16[16,16,4,1024]{3,2,1,0:T(4,128)(2,1)S(1)}, u32[]{:S(2)}, u32[]{:S(2)}) async-start(bf16[16,16,4,1024]{3,2,1,0:T(4,128)(2,1)} %bitcast.120), calls=%async_computation.1 | async-start | bytes 4194304 | tf_op jit(solution)/shard_map/all_to_all | solution.py:137
  67.8 139.7 %all-gather.5.cloned.1.call-start = ((), (), s32[]{:S(2)}) async-start(), calls=%async_computation.5 | async-start | bytes 2162688 | tf_op jit(solution)/shard_map/all_gather | solution.py:38
  70.0 5.1 %collective-permute-start = (bf16[3,192,1024]{2,1,0:T(8,128)(2,1)}, bf16[3,192,1024]{2,1,0:T(8,128)(2,1)}, u32[]{:S(2)}, u32[]{:S(2)}) collective-permute-start(bf16[3,192,1024]{2,1,0:T(8,128)(2,1)} %pad_maximum_fusion), channel_id=1, source_target_pairs={{0,1},{1,0},{2,3},{3,2},{4,5},{5,4},{6,7},{7,6},{8,9},{9,8},{10,11... | collective-permute-start | bytes 3538952 | tf_op jit(solution)/shard_map/ppermute | solution.py:9
  117.2 3.2 %copy-start.2 = (bf16[3,384,1024]{2,1,0:T(8,128)(2,1)S(1)}, bf16[3,384,1024]{2,1,0:T(8,128)(2,1)}, u32[]{:S(2)}) copy-start(bf16[3,384,1024]{2,1,0:T(8,128)(2,1)} %maximum_select_fusion) | copy-start | bytes 7077892
  117.2 3.2 %copy-start.3 = (bf16[1024,1024]{1,0:T(8,128)(2,1)S(1)}, bf16[1024,1024]{1,0:T(8,128)(2,1)}, u32[]{:S(2)}) copy-start(bf16[1024,1024]{1,0:T(8,128)(2,1)} %reshape.284) | copy-start | bytes 6291460
  128.8 8.1 %copy-start.9 = (s32[1,128,2]{1,2,0:T(2,128)S(1)}, s32[1,128,2]{1,2,0:T(2,128)}, u32[]{:S(2)}) copy-start(s32[1,128,2]{1,2,0:T(2,128)} %param.16) | copy-start | bytes 3076
  128.8 54.1 %all-to-all-start.2 = ((bf16[16,16,4,1024]{3,1,2,0:T(8,128)(2,1)}), bf16[16,16,4,1024]{3,1,2,0:T(8,128)(2,1)S(1)}, u32[]{:S(2)}, u32[]{:S(2)}) async-start(bf16[16,16,4,1024]{3,1,2,0:T(8,128)(2,1)} %convolution_convert_fusion), calls=%async_computation.2 | async-start | bytes 4194304 | tf_op jit(solution)/shard_map/all_to_all | solution.py:139
  185.9 21.5 %copy-start.6 = (f32[2,8,128,128]{3,2,1,0:T(8,128)S(1)}, f32[2,8,128,128]{3,2,1,0:T(8,128)}, u32[]{:S(2)}) copy-start(f32[2,8,128,128]{3,2,1,0:T(8,128)} %custom-call.4) | copy-start | bytes 3145732
  187.7 110.8 %all-to-all-start.3 = ((bf16[4,32,4,1024]{3,2,0,1:T(4,128)(2,1)}), bf16[4,32,4,1024]{3,2,0,1:T(4,128)(2,1)S(1)}, u32[]{:S(2)}, u32[]{:S(2)}) async-start(bf16[4,32,4,1024]{3,2,0,1:T(4,128)(2,1)} %copy.88), calls=%async_computation.3 | async-start | bytes 2097152 | tf_op jit(solution)/shard_map/all_to_all | solution.py:146
  212.5 3.4 %copy-start.1 = (f32[2,512,128,8]{2,1,3,0:T(8,128)S(1)}, f32[2,512,128,8]{2,1,3,0:T(8,128)}, u32[]{:S(2)}) copy-start(f32[2,512,128,8]{2,1,3,0:T(8,128)} %get-tuple-element.203) | copy-start | bytes 12582916 | tf_op jit(solution)/shard_map/while
  223.7 3.4 %copy-start.1 = (f32[2,512,128,8]{2,1,3,0:T(8,128)S(1)}, f32[2,512,128,8]{2,1,3,0:T(8,128)}, u32[]{:S(2)}) copy-start(f32[2,512,128,8]{2,1,3,0:T(8,128)} %get-tuple-element.203) | copy-start | bytes 12582916 | tf_op jit(solution)/shard_map/while
  234.9 3.4 %copy-start.1 = (f32[2,512,128,8]{2,1,3,0:T(8,128)S(1)}, f32[2,512,128,8]{2,1,3,0:T(8,128)}, u32[]{:S(2)}) copy-start(f32[2,512,128,8]{2,1,3,0:T(8,128)} %get-tuple-element.203) | copy-start | bytes 12582916 | tf_op jit(solution)/shard_map/while
  246.1 3.4 %copy-start.1 = (f32[2,512,128,8]{2,1,3,0:T(8,128)S(1)}, f32[2,512,128,8]{2,1,3,0:T(8,128)}, u32[]{:S(2)}) copy-start(f32[2,512,128,8]{2,1,3,0:T(8,128)} %get-tuple-element.203) | copy-start | bytes 12582916 | tf_op jit(solution)/shard_map/while
  257.3 3.4 %copy-start.1 = (f32[2,512,128,8]{2,1,3,0:T(8,128)S(1)}, f32[2,512,128,8]{2,1,3,0:T(8,128)}, u32[]{:S(2)}) copy-start(f32[2,512,128,8]{2,1,3,0:T(8,128)} %get-tuple-element.203) | copy-start | bytes 12582916 | tf_op jit(solution)/shard_map/while
  268.5 3.4 %copy-start.1 = (f32[2,512,128,8]{2,1,3,0:T(8,128)S(1)}, f32[2,512,128,8]{2,1,3,0:T(8,128)}, u32[]{:S(2)}) copy-start(f32[2,512,128,8]{2,1,3,0:T(8,128)} %get-tuple-element.203) | copy-start | bytes 12582916 | tf_op jit(solution)/shard_map/while
  279.7 3.4 %copy-start.1 = (f32[2,512,128,8]{2,1,3,0:T(8,128)S(1)}, f32[2,512,128,8]{2,1,3,0:T(8,128)}, u32[]{:S(2)}) copy-start(f32[2,512,128,8]{2,1,3,0:T(8,128)} %get-tuple-element.203) | copy-start | bytes 12582916 | tf_op jit(solution)/shard_map/while
  290.9 3.4 %copy-start.1 = (f32[2,512,128,8]{2,1,3,0:T(8,128)S(1)}, f32[2,512,128,8]{2,1,3,0:T(8,128)}, u32[]{:S(2)}) copy-start(f32[2,512,128,8]{2,1,3,0:T(8,128)} %get-tuple-element.203) | copy-start | bytes 12582916 | tf_op jit(solution)/shard_map/while
Sparse Core Ops, SparseCore 0:
  34.1 84.8 all-gather.2
  122.8 84.6 all-gather.4
where the time goes:
time: 311 us; the launch traced here: 310 us
  waiting for transfers between devices  124 us (40%)
  matrix products  60 us (19%)
  other arithmetic  41.4 us (13%)
  starting transfers between devices  34.9 us (11%)
  local copies, waits for them, and re-layouts  29.7 us (10%)
  between operations  14.4 us (5%)
  loops' own time  5.69 us (2%)
    all_to_all x1, waiting for transfers between devices, local(): lax.all_to_all(partials.astype(jnp.bfloat16), 'exp', split_axis=0, concat...  43 us
    all_to_all x1, waiting for transfers between devices, local(): lax.all_to_all(spread_rows, 'exp', split_axis=0, concat_axis=0, tiled=True)  36.6 us
    dot_general x8, matrix products, advance(): jnp.einsum('qhgd,khd->hgqk', grouped, key_block, preferred_element_type=j...  29.5 us
    all_to_all x1, waiting for transfers between devices, local(): lax.all_to_all(outgoing, 'ctx', split_axis=1, concat_axis=1, tiled=True)  27.4 us
    reduce_sum x8, other arithmetic, advance(): totals = totals * factor + jnp.sum(weights, axis=-1)  26.6 us
    dot_general x8, matrix products, advance(): jnp.einsum('hgqk,khd->hgqd', weights.astype(jnp.bfloat16), value_block, p...  21.1 us
    all_gather x1, waiting for transfers between devices, attention(): value_piece = lax.all_gather(value_rows, 'ctx', axis=1, tiled=True)  14.3 us
    all_to_all x1, starting transfers between devices, local(): lax.all_to_all(outgoing, 'ctx', split_axis=1, concat_axis=1, tiled=True)  13.2 us
  transfers between devices with their start and end apart: 7, of which 5 were waited for; matrix products, arithmetic and copies ran while one was open for 38% of the time, Pallas kernels for 0%

commit v1 on v0

--- a/solution.py
+++ b/solution.py
@@ -35,7 +35,9 @@
         jnp.zeros((kv_count, group_size, seq_rows, head_size), jnp.float32),
     )
     key_piece = lax.all_gather(key_rows, "ctx", axis=1, tiled=True)
-    value_piece = lax.all_gather(value_rows, "ctx", axis=1, tiled=True)
+    value_piece = jnp.concatenate(
+        lax.all_to_all(jnp.stack([value_rows] * lax.axis_size("ctx")), "ctx", 0, 0), axis=1
+    )
     piece_rows = key_piece.shape[1]
     block_rows = math.gcd(piece_rows, 512)
     block_count = piece_rows // block_rows

time: 311 us -> 344 us (1.11)
  the two profiles are of different devices: /device:TPU:16 before, /device:TPU:1 now
where the time goes in v1:
time: 344 us; the launch traced here: 343 us
  waiting for transfers between devices  116 us (34%)
  matrix products  61.4 us (18%)
  other arithmetic  42.5 us (12%)
  blocking collectives  39.7 us (12%)
  local copies, waits for them, and re-layouts  32.2 us (9%)
  starting transfers between devices  30.6 us (9%)
  between operations  14.4 us (4%)
  loops' own time  5.71 us (2%)
    all_to_all x1, waiting for transfers between devices, local(): lax.all_to_all(spread_rows, 'exp', split_axis=0, concat_axis=0, tiled=True)  48.9 us
    all_to_all x1, waiting for transfers between devices, local(): lax.all_to_all(partials.astype(jnp.bfloat16), 'exp', split_axis=0, concat...  43.2 us
    all_to_all x1, blocking collectives, local(): lax.all_to_all(outgoing, 'ctx', split_axis=1, concat_axis=1, tiled=True)  39.7 us
    dot_general x8, matrix products, advance(): jnp.einsum('qhgd,khd->hgqk', grouped, key_block, preferred_element_type=j...  29.5 us
    reduce_sum x8, other arithmetic, advance(): totals = totals * factor + jnp.sum(weights, axis=-1)  26.6 us
    all_to_all x1, waiting for transfers between devices, attention(): lax.all_to_all(jnp.stack([value_rows] * lax.axis_size('ctx')), 'ctx', 0, 0)  22 us
    dot_general x8, matrix products, advance(): jnp.einsum('hgqk,khd->hgqd', weights.astype(jnp.bfloat16), value_block, p...  21.1 us
    all_to_all x1, starting transfers between devices, local(): lax.all_to_all(spread_rows, 'exp', split_axis=0, concat_axis=0, tiled=True)  10.1 us
  transfers between devices with their start and end apart: 6, of which 4 were waited for; matrix products, arithmetic and copies ran while one was open for 35% of the time, Pallas kernels for 0%

profile of v1, /device:TPU:1, one launch (start us, length us, event | category | flops | bytes accessed | tf_op | source)
XLA Modules:
  0.0 342.9 jit_solution(2159745696000030054)
XLA Ops:
  15.3 39.7 %all_to_all.25 = bf16[4,32,4,1024]{3,2,0,1:T(4,128)(2,1)S(1)} all-to-all(bf16[4,32,4,1024]{3,2,0,1:T(4,128)(2,1)S(1)} %copy.87), channel_id=1, replica_groups=mesh['ctx'=32,'exp'=16] {'ctx'}, dimensions={1} | all-to-all | bytes 2097152 | tf_op jit(solution)/shard_map/all_to_all | solution.py:123
  57.6 10.1 %all-to-all-start.2 = ((bf16[16,16,4,1024]{3,2,1,0:T(4,128)(2,1)}), bf16[16,16,4,1024]{3,2,1,0:T(4,128)(2,1)S(1)}, u32[]{:S(2)}, u32[]{:S(2)}) async-start(bf16[16,16,4,1024]{3,2,1,0:T(4,128)(2,1)} %bitcast.120), calls=%async_computation.2 | async-start | bytes 4194304 | tf_op jit(solution)/shard_map/all_to_all | solution.py:139
  67.7 48.9 %all-to-all-done.2 = bf16[16,16,4,1024]{3,2,1,0:T(4,128)(2,1)S(1)} async-done(((bf16[16,16,4,1024]{3,2,1,0:T(4,128)(2,1)}), bf16[16,16,4,1024]{3,2,1,0:T(4,128)(2,1)S(1)}, u32[]{:S(2)}, u32[]{:S(2)}) %all-to-all-start.2) | async-done | bytes 2097184 | tf_op jit(solution)/shard_map/all_to_all | solution.py:139
  118.6 5.4 %all-to-all-start = ((bf16[32,1,128,2,128]{4,2,3,1,0:T(8,128)(2,1)}), bf16[32,1,128,2,128]{4,2,3,1,0:T(8,128)(2,1)S(1)}, u32[]{:S(2)}, u32[]{:S(2)}) async-start(bf16[32,1,128,2,128]{4,2,3,1,0:T(8,128)(2,1)} %stack.10), calls=%async_computation | async-start | bytes 4194304 | tf_op jit(solution)/shard_map/all_to_all | solution.py:39
  131.8 3.9 %maximum_select_fusion = bf16[3,384,1024]{2,1,0:T(8,128)(2,1)} fusion(bf16[1,192,1024]{2,1,0:T(8,128)(2,1)S(1)} %bitcast.125, bf16[1,192,1024]{2,1,0:T(8,128)(2,1)} %bitcast.127, bf16[1,192,1024]{2,1,0:T(8,128)(2,1)} %bitcast.129, bf16[3,192,1024]{2,1,0:T(8,128)(2,1)} %collective-permute-done, pred[]{:T(512)S(6)} %eq.35), kind=kLoop, calls=%fused_computation.30 | loop fusion | flops 20054016 | bytes 4718593 | tf_op jit(solution)/shard_map/jit(_where)/select_n | solution.py:128
  135.7 4.0 %reshape.287 = bf16[1024,1024]{1,0:T(8,128)(2,1)} reshape(bf16[16,16,4,1024]{3,2,1,0:T(4,128)(2,1)} %copy-done.2) | data formatting | bytes 4194304 | tf_op jit(solution)/shard_map/reshape | solution.py:14
  142.9 3.4 multiply_convert_fusion
  148.7 4.0 %convolution_convert_fusion = bf16[16,16,4,1024]{3,1,2,0:T(8,128)(2,1)} fusion(bf16[3,384,1024]{2,1,0:T(8,128)(2,1)} %maximum_select_fusion, bf16[16,16,4,384]{3,2,1,0:T(4,128)(2,1)} %dot_general.22), kind=kOutput, calls=%fused_computation.31 | convolution fusion | flops 806354944 | bytes 3670016 | tf_op jit(solution)/shard_map/dot_general | solution.py:19
  152.7 22.0 %all-to-all-done = bf16[32,1,128,2,128]{4,2,3,1,0:T(8,128)(2,1)S(1)} async-done(((bf16[32,1,128,2,128]{4,2,3,1,0:T(8,128)(2,1)}), bf16[32,1,128,2,128]{4,2,3,1,0:T(8,128)(2,1)S(1)}, u32[]{:S(2)}, u32[]{:S(2)}) %all-to-all-start) | async-done | bytes 2097184 | tf_op jit(solution)/shard_map/all_to_all | solution.py:39
  174.7 7.4 %all-to-all-start.3 = ((bf16[16,16,4,1024]{3,1,2,0:T(8,128)(2,1)}), bf16[16,16,4,1024]{3,1,2,0:T(8,128)(2,1)}, u32[]{:S(2)}, u32[]{:S(2)}) async-start(bf16[16,16,4,1024]{3,1,2,0:T(8,128)(2,1)} %convolution_convert_fusion), calls=%async_computation.3 | async-start | bytes 4194304 | tf_op jit(solution)/shard_map/all_to_all | solution.py:141
  188.0 43.2 %all-to-all-done.3 = bf16[16,16,4,1024]{3,1,2,0:T(8,128)(2,1)} async-done(((bf16[16,16,4,1024]{3,1,2,0:T(8,128)(2,1)}), bf16[16,16,4,1024]{3,1,2,0:T(8,128)(2,1)}, u32[]{:S(2)}, u32[]{:S(2)}) %all-to-all-start.3) | async-done | bytes 2097184 | tf_op jit(solution)/shard_map/all_to_all | solution.py:141
  235.3 5.1 %all-to-all-start.4 = ((bf16[4,32,4,1024]{3,2,0,1:T(4,128)(2,1)}), bf16[4,32,4,1024]{3,2,0,1:T(4,128)(2,1)S(1)}, u32[]{:S(2)}, u32[]{:S(2)}) async-start(bf16[4,32,4,1024]{3,2,0,1:T(4,128)(2,1)} %copy.91), calls=%async_computation.4 | async-start | bytes 2097152 | tf_op jit(solution)/shard_map/all_to_all | solution.py:148
  240.5 89.6 %while.15 = (s32[]{:T(128)}, f32[2,8,128]{2,1,0:T(8,128)S(1)}, f32[2,8,128]{2,1,0:T(8,128)S(1)}, f32[2,8,128,128]{3,2,1,0:T(8,128)S(1)}, s32[8]{0:T(128)S(1)}, /...) while((s32[]{:T(128)}, f32[2,8,128]{2,1,0:T(8,128)S(1)}, ...), condition=%wide.region_3.4_spmd.clone, body=%wide.region_0.3_spmd.clone.sunk | while | flops 551365248 | bytes 32904396 | solution.py:69
  241.9 3.7 %fusion.58 = (f32[2,8,128]{2,1,0:T(8,128)S(1)}, f32[2,512,128,8]{2,1,3,0:T(8,128)}) fusion(pred[128,512]{0,1:T(8,128)(4,1)S(1)} %broadcast_compare_fusion.2, bf16[128,2,8,128]{3,0,2,1:T(8,128)(2,1)S(1)} %get-tuple-element.236, bf16[8,512,2,128]{3,1,0,2:T(8,128)(2,1)} %get-tuple-element.235, s32[]{:T(128)S(6)} %copy.110), kind=kOutput, calls=%fused_computation.6.clone.1 | convolution fusion | flops 271579136 | bytes 5054468 | tf_op jit(solution)/shard_map/while/body/eval_jaxpr/qhgd,khd->hgqk/dot_general | solution.py:51
  245.6 3.3 fusion.59
  253.1 3.7 %fusion.58 = (f32[2,8,128]{2,1,0:T(8,128)S(1)}, f32[2,512,128,8]{2,1,3,0:T(8,128)}) fusion(pred[128,512]{0,1:T(8,128)(4,1)S(1)} %broadcast_compare_fusion.2, bf16[128,2,8,128]{3,0,2,1:T(8,128)(2,1)S(1)} %get-tuple-element.236, bf16[8,512,2,128]{3,1,0,2:T(8,128)(2,1)} %get-tuple-element.235, s32[]{:T(128)S(6)} %copy.110), kind=kOutput, calls=%fused_computation.6.clone.1 | convolution fusion | flops 271579136 | bytes 5054468 | tf_op jit(solution)/shard_map/while/body/eval_jaxpr/qhgd,khd->hgqk/dot_general | solution.py:51
  256.8 3.3 fusion.59
  264.3 3.7 %fusion.58 = (f32[2,8,128]{2,1,0:T(8,128)S(1)}, f32[2,512,128,8]{2,1,3,0:T(8,128)}) fusion(pred[128,512]{0,1:T(8,128)(4,1)S(1)} %broadcast_compare_fusion.2, bf16[128,2,8,128]{3,0,2,1:T(8,128)(2,1)S(1)} %get-tuple-element.236, bf16[8,512,2,128]{3,1,0,2:T(8,128)(2,1)} %get-tuple-element.235, s32[]{:T(128)S(6)} %copy.110), kind=kOutput, calls=%fused_computation.6.clone.1 | convolution fusion | flops 271579136 | bytes 5054468 | tf_op jit(solution)/shard_map/while/body/eval_jaxpr/qhgd,khd->hgqk/dot_general | solution.py:51
  268.0 3.3 fusion.59
  275.5 3.7 %fusion.58 = (f32[2,8,128]{2,1,0:T(8,128)S(1)}, f32[2,512,128,8]{2,1,3,0:T(8,128)}) fusion(pred[128,512]{0,1:T(8,128)(4,1)S(1)} %broadcast_compare_fusion.2, bf16[128,2,8,128]{3,0,2,1:T(8,128)(2,1)S(1)} %get-tuple-element.236, bf16[8,512,2,128]{3,1,0,2:T(8,128)(2,1)} %get-tuple-element.235, s32[]{:T(128)S(6)} %copy.110), kind=kOutput, calls=%fused_computation.6.clone.1 | convolution fusion | flops 271579136 | bytes 5054468 | tf_op jit(solution)/shard_map/while/body/eval_jaxpr/qhgd,khd->hgqk/dot_general | solution.py:51
  286.7 3.7 %fusion.58 = (f32[2,8,128]{2,1,0:T(8,128)S(1)}, f32[2,512,128,8]{2,1,3,0:T(8,128)}) fusion(pred[128,512]{0,1:T(8,128)(4,1)S(1)} %broadcast_compare_fusion.2, bf16[128,2,8,128]{3,0,2,1:T(8,128)(2,1)S(1)} %get-tuple-element.236, bf16[8,512,2,128]{3,1,0,2:T(8,128)(2,1)} %get-tuple-element.235, s32[]{:T(128)S(6)} %copy.110), kind=kOutput, calls=%fused_computation.6.clone.1 | convolution fusion | flops 271579136 | bytes 5054468 | tf_op jit(solution)/shard_map/while/body/eval_jaxpr/qhgd,khd->hgqk/dot_general | solution.py:51
  297.9 3.7 %fusion.58 = (f32[2,8,128]{2,1,0:T(8,128)S(1)}, f32[2,512,128,8]{2,1,3,0:T(8,128)}) fusion(pred[128,512]{0,1:T(8,128)(4,1)S(1)} %broadcast_compare_fusion.2, bf16[128,2,8,128]{3,0,2,1:T(8,128)(2,1)S(1)} %get-tuple-element.236, bf16[8,512,2,128]{3,1,0,2:T(8,128)(2,1)} %get-tuple-element.235, s32[]{:T(128)S(6)} %copy.110), kind=kOutput, calls=%fused_computation.6.clone.1 | convolution fusion | flops 271579136 | bytes 5054468 | tf_op jit(solution)/shard_map/while/body/eval_jaxpr/qhgd,khd->hgqk/dot_general | solution.py:51
  309.1 3.7 %fusion.58 = (f32[2,8,128]{2,1,0:T(8,128)S(1)}, f32[2,512,128,8]{2,1,3,0:T(8,128)}) fusion(pred[128,512]{0,1:T(8,128)(4,1)S(1)} %broadcast_compare_fusion.2, bf16[128,2,8,128]{3,0,2,1:T(8,128)(2,1)S(1)} %get-tuple-element.236, bf16[8,512,2,128]{3,1,0,2:T(8,128)(2,1)} %get-tuple-element.235, s32[]{:T(128)S(6)} %copy.110), kind=kOutput, calls=%fused_computation.6.clone.1 | convolution fusion | flops 271579136 | bytes 5054468 | tf_op jit(solution)/shard_map/while/body/eval_jaxpr/qhgd,khd->hgqk/dot_general | solution.py:51
  320.3 3.7 %fusion.58 = (f32[2,8,128]{2,1,0:T(8,128)S(1)}, f32[2,512,128,8]{2,1,3,0:T(8,128)}) fusion(pred[128,512]{0,1:T(8,128)(4,1)S(1)} %broadcast_compare_fusion.2, bf16[128,2,8,128]{3,0,2,1:T(8,128)(2,1)S(1)} %get-tuple-element.236, bf16[8,512,2,128]{3,1,0,2:T(8,128)(2,1)} %get-tuple-element.235, s32[]{:T(128)S(6)} %copy.110), kind=kOutput, calls=%fused_computation.6.clone.1 | convolution fusion | flops 271579136 | bytes 5054468 | tf_op jit(solution)/shard_map/while/body/eval_jaxpr/qhgd,khd->hgqk/dot_general | solution.py:51
  (168 shorter events, 86.1 us)
Async XLA Ops:
  7.2 176.9 %copy-start = (bf16[1024,128]{1,0:T(8,128)(2,1)S(1)}, bf16[1024,128]{1,0:T(8,128)(2,1)}, u32[]{:S(2)}) copy-start(bf16[1024,128]{1,0:T(8,128)(2,1)} %param.18) | copy-start | bytes 786436
  57.6 10.1 %copy-start.6 = (bf16[1,128,2,128]{3,2,1,0:T(2,128)(2,1)S(1)}, bf16[1,128,2,128]{3,2,1,0:T(2,128)(2,1)}, u32[]{:S(2)}) copy-start(bf16[1,128,2,128]{3,2,1,0:T(2,128)(2,1)} %param.15) | copy-start | bytes 196612
  57.6 59.0 %all-to-all-start.2 = ((bf16[16,16,4,1024]{3,2,1,0:T(4,128)(2,1)}), bf16[16,16,4,1024]{3,2,1,0:T(4,128)(2,1)S(1)}, u32[]{:S(2)}, u32[]{:S(2)}) async-start(bf16[16,16,4,1024]{3,2,1,0:T(4,128)(2,1)} %bitcast.120), calls=%async_computation.2 | async-start | bytes 4194304 | tf_op jit(solution)/shard_map/all_to_all | solution.py:139
  116.6 2.0 copy-start.2
  118.6 10.4 %copy-start.7 = (bf16[1,128,2,128]{3,2,1,0:T(2,128)(2,1)S(1)}, bf16[1,128,2,128]{3,2,1,0:T(2,128)(2,1)}, u32[]{:S(2)}) copy-start(bf16[1,128,2,128]{3,2,1,0:T(2,128)(2,1)} %param.14) | copy-start | bytes 196612
  118.6 56.1 %all-to-all-start = ((bf16[32,1,128,2,128]{4,2,3,1,0:T(8,128)(2,1)}), bf16[32,1,128,2,128]{4,2,3,1,0:T(8,128)(2,1)S(1)}, u32[]{:S(2)}, u32[]{:S(2)}) async-start(bf16[32,1,128,2,128]{4,2,3,1,0:T(8,128)(2,1)} %stack.10), calls=%async_computation | async-start | bytes 4194304 | tf_op jit(solution)/shard_map/all_to_all | solution.py:39
  124.0 7.8 %copy-start.4 = (bf16[192,1024]{1,0:T(8,128)(2,1)S(1)}, bf16[192,1024]{1,0:T(8,128)(2,1)}, u32[]{:S(2)}) copy-start(bf16[192,1024]{1,0:T(8,128)(2,1)} %param.21) | copy-start | bytes 1179652
  124.0 116.5 %all-gather.2.cloned.1.call-start = ((), (), s32[]{:S(2)}) async-start(), calls=%async_computation.5 | async-start | bytes 2162688 | tf_op jit(solution)/shard_map/all_gather | solution.py:37
  126.5 5.3 %collective-permute-start = (bf16[3,192,1024]{2,1,0:T(8,128)(2,1)}, bf16[3,192,1024]{2,1,0:T(8,128)(2,1)}, u32[]{:S(2)}, u32[]{:S(2)}) collective-permute-start(bf16[3,192,1024]{2,1,0:T(8,128)(2,1)} %pad_maximum_fusion), channel_id=1, source_target_pairs={{0,1},{1,0},{2,3},{3,2},{4,5},{5,4},{6,7},{7,6},{8,9},{9,8},{10,11... | collective-permute-start | bytes 3538952 | tf_op jit(solution)/shard_map/ppermute | solution.py:9
  139.7 3.2 copy-start.3
  152.7 30.9 %copy-start.8 = (s32[1,128,2]{1,2,0:T(2,128)S(1)}, s32[1,128,2]{1,2,0:T(2,128)}, u32[]{:S(2)}) copy-start(s32[1,128,2]{1,2,0:T(2,128)} %param.16) | copy-start | bytes 3076
  174.7 56.5 %all-to-all-start.3 = ((bf16[16,16,4,1024]{3,1,2,0:T(8,128)(2,1)}), bf16[16,16,4,1024]{3,1,2,0:T(8,128)(2,1)}, u32[]{:S(2)}, u32[]{:S(2)}) async-start(bf16[16,16,4,1024]{3,1,2,0:T(8,128)(2,1)} %convolution_convert_fusion), calls=%async_computation.3 | async-start | bytes 4194304 | tf_op jit(solution)/shard_map/all_to_all | solution.py:141
  233.5 6.9 %copy-start.5 = (f32[2,8,128,128]{3,2,1,0:T(8,128)S(1)}, f32[2,8,128,128]{3,2,1,0:T(8,128)}, u32[]{:S(2)}) copy-start(f32[2,8,128,128]{3,2,1,0:T(8,128)} %custom-call.4) | copy-start | bytes 3145732
  235.3 96.3 %all-to-all-start.4 = ((bf16[4,32,4,1024]{3,2,0,1:T(4,128)(2,1)}), bf16[4,32,4,1024]{3,2,0,1:T(4,128)(2,1)S(1)}, u32[]{:S(2)}, u32[]{:S(2)}) async-start(bf16[4,32,4,1024]{3,2,0,1:T(4,128)(2,1)} %copy.91), calls=%async_computation.4 | async-start | bytes 2097152 | tf_op jit(solution)/shard_map/all_to_all | solution.py:148
  245.6 3.4 %copy-start.1 = (f32[2,512,128,8]{2,1,3,0:T(8,128)S(1)}, f32[2,512,128,8]{2,1,3,0:T(8,128)}, u32[]{:S(2)}) copy-start(f32[2,512,128,8]{2,1,3,0:T(8,128)} %get-tuple-element.203) | copy-start | bytes 12582916 | tf_op jit(solution)/shard_map/while
  256.8 3.4 %copy-start.1 = (f32[2,512,128,8]{2,1,3,0:T(8,128)S(1)}, f32[2,512,128,8]{2,1,3,0:T(8,128)}, u32[]{:S(2)}) copy-start(f32[2,512,128,8]{2,1,3,0:T(8,128)} %get-tuple-element.203) | copy-start | bytes 12582916 | tf_op jit(solution)/shard_map/while
  268.0 3.4 %copy-start.1 = (f32[2,512,128,8]{2,1,3,0:T(8,128)S(1)}, f32[2,512,128,8]{2,1,3,0:T(8,128)}, u32[]{:S(2)}) copy-start(f32[2,512,128,8]{2,1,3,0:T(8,128)} %get-tuple-element.203) | copy-start | bytes 12582916 | tf_op jit(solution)/shard_map/while
  279.2 3.4 %copy-start.1 = (f32[2,512,128,8]{2,1,3,0:T(8,128)S(1)}, f32[2,512,128,8]{2,1,3,0:T(8,128)}, u32[]{:S(2)}) copy-start(f32[2,512,128,8]{2,1,3,0:T(8,128)} %get-tuple-element.203) | copy-start | bytes 12582916 | tf_op jit(solution)/shard_map/while
  290.4 3.4 %copy-start.1 = (f32[2,512,128,8]{2,1,3,0:T(8,128)S(1)}, f32[2,512,128,8]{2,1,3,0:T(8,128)}, u32[]{:S(2)}) copy-start(f32[2,512,128,8]{2,1,3,0:T(8,128)} %get-tuple-element.203) | copy-start | bytes 12582916 | tf_op jit(solution)/shard_map/while
  301.6 3.4 %copy-start.1 = (f32[2,512,128,8]{2,1,3,0:T(8,128)S(1)}, f32[2,512,128,8]{2,1,3,0:T(8,128)}, u32[]{:S(2)}) copy-start(f32[2,512,128,8]{2,1,3,0:T(8,128)} %get-tuple-element.203) | copy-start | bytes 12582916 | tf_op jit(solution)/shard_map/while
  312.8 3.4 %copy-start.1 = (f32[2,512,128,8]{2,1,3,0:T(8,128)S(1)}, f32[2,512,128,8]{2,1,3,0:T(8,128)}, u32[]{:S(2)}) copy-start(f32[2,512,128,8]{2,1,3,0:T(8,128)} %get-tuple-element.203) | copy-start | bytes 12582916 | tf_op jit(solution)/shard_map/while
  324.0 3.4 %copy-start.1 = (f32[2,512,128,8]{2,1,3,0:T(8,128)S(1)}, f32[2,512,128,8]{2,1,3,0:T(8,128)}, u32[]{:S(2)}) copy-start(f32[2,512,128,8]{2,1,3,0:T(8,128)} %get-tuple-element.203) | copy-start | bytes 12582916 | tf_op jit(solution)/shard_map/while
Sparse Core Ops, SparseCore 0:
  129.8 85.6 all-gather.1
